TPU v7x, 256 devices: a whole 4x4x8 slice. The times are simulated.
256 devices in a mesh: uly: 8 (over x_hi, y), blk: 32 (over x_lo, z, core).
Axes of the slice: x: 4 (x_hi: 2, x_lo: 2; x = x_hi * 2 + x_lo), y: 4, z: 8, core: 2. Of those that a mesh axis runs over, the one named last changes fastest.
Arguments:
- queries: bfloat16 [16384, 2048], P(('uly', 'blk')), may hold values from -6 to 6
- key_vector_rows: bfloat16 [16384, 256], P(('uly', 'blk')), may hold values from -6 to 6
- value_vector_rows: bfloat16 [16384, 256], P(('uly', 'blk')), may hold values from -6 to 6
- out_grad: bfloat16 [16384, 2048], P(('uly', 'blk')), may hold values from -6 to 6
- block_list: int32 [16, 128, 8], P('uly'), may hold values from 0 to 127, as said below
Outputs:
- attended: bfloat16 [16384, 2048], P(('uly', 'blk'))
- query_grad: bfloat16 [16384, 2048], P(('uly', 'blk'))
- gradient_keys: bfloat16 [16384, 256], P(('uly', 'blk'))
- gradient_values: bfloat16 [16384, 256], P(('uly', 'blk'))
Inputs may be any that keep to these rules, and one draw needn't show every extreme that they name: block_list[h, i] names key blocks for query block i of head h: its first entry is always i itself, every entry is at most i, and a block may be named several times.
All inputs are finite; a program needn't handle non-finite values.
Results may differ from a plain program's by a relative error of at most 0.039.
Values may be sent and summed in bfloat16 or wider, within the bound.
No kernel may reach another device: no remote copies, remote signals or barrier semaphores. Data moves between devices by JAX's collectives and lax.ppermute only.
A program may use at most 128 MiB of HBM per device.

v0:
```python
import math
import jax
import jax.numpy as jnp
from jax import lax
from jax.sharding import PartitionSpec as P

KEY_VALUE_HEADS = 2
HEAD_SIZE = 128
BLOCK = 128


def body(queries, key_vector_rows, value_vector_rows, out_grad, block_list):
    ulysses_width = lax.axis_size("uly")
    cycle_size = lax.axis_size("blk")
    segment_length = queries.shape[0]
    heads_dev = block_list.shape[0]
    list_len = block_list.shape[2]
    head_width = heads_dev * HEAD_SIZE
    copy_count = ulysses_width // KEY_VALUE_HEADS
    cycle_index = lax.axis_index("blk")
    score_scale = 1.0 / math.sqrt(HEAD_SIZE)
    sub_length = min(segment_length, BLOCK)
    sub_count = segment_length // sub_length
    unit_len = min(segment_length, BLOCK)
    units_per_block = BLOCK // unit_len
    units_per_segment = segment_length // unit_len
    total_tokens = segment_length * ulysses_width * cycle_size
    units_total = total_tokens // unit_len
    query_slots = queries.reshape(segment_length, ulysses_width, head_width)
    grad_slots = out_grad.reshape(segment_length, ulysses_width, head_width)
    kv_local = jnp.concatenate(
        [
            key_vector_rows.reshape(segment_length, KEY_VALUE_HEADS, HEAD_SIZE),
            value_vector_rows.reshape(segment_length, KEY_VALUE_HEADS, HEAD_SIZE),
        ],
        axis=2,
    )
    kv_slots = jnp.repeat(kv_local, copy_count, axis=1)
    query_all, kv_mine, grad_all = (
        lax.all_to_all(query_slots, "uly", split_axis=1, concat_axis=0, tiled=True),
        lax.all_to_all(kv_slots, "uly", split_axis=1, concat_axis=0, tiled=True),
        lax.all_to_all(grad_slots, "uly", split_axis=1, concat_axis=0, tiled=True),
    )
    keys_all = lax.all_gather(kv_mine[:, 0, :], "blk", axis=0, tiled=True)
    item_count = heads_dev * ulysses_width * sub_count
    query_items = (
        query_all.reshape(ulysses_width, sub_count, sub_length, heads_dev, HEAD_SIZE)
        .transpose(3, 0, 1, 2, 4)
        .reshape(item_count, sub_length, HEAD_SIZE)
    )
    grad_items = (
        grad_all.reshape(ulysses_width, sub_count, sub_length, heads_dev, HEAD_SIZE)
        .transpose(3, 0, 1, 2, 4)
        .reshape(item_count, sub_length, HEAD_SIZE)
    )
    item_ids = jnp.arange(item_count, dtype=jnp.int32)
    head_ids = item_ids // (ulysses_width * sub_count)
    slot_ids = item_ids // sub_count % ulysses_width
    sub_ids = item_ids % sub_count
    segments = slot_ids * cycle_size + cycle_index
    first_pos = segments * segment_length + sub_ids * sub_length
    query_block = first_pos // BLOCK
    entries = block_list[head_ids, query_block]
    earlier = jnp.arange(list_len)[:, None] > jnp.arange(list_len)[None, :]
    repeated = jnp.any((entries[:, :, None] == entries[:, None, :]) & earlier[None, :, :], axis=2)
    offsets = jnp.arange(BLOCK, dtype=jnp.int32)
    key_pos = (entries[:, :, None] * BLOCK + offsets[None, None, :]).reshape(
        item_count, list_len * BLOCK
    )
    live_keys = jnp.repeat(jnp.logical_not(repeated), BLOCK, axis=1)
    query_pos = first_pos[:, None] + jnp.arange(sub_length, dtype=jnp.int32)[None, :]
    allowed = (key_pos[:, None, :] <= query_pos[:, :, None]) & live_keys[:, None, :]
    unit_count = list_len * units_per_block
    natural_units = (
        entries[:, :, None] * units_per_block
        + jnp.arange(units_per_block, dtype=jnp.int32)[None, None, :]
    ).reshape(item_count, unit_count)
    unit_seg = natural_units // units_per_segment
    canon_units = (
        unit_seg % cycle_size * ulysses_width + unit_seg // cycle_size
    ) * units_per_segment + natural_units % units_per_segment
    keys_units = keys_all.reshape(units_total, unit_len * 2 * HEAD_SIZE)
    unit_iota = jnp.arange(units_total, dtype=jnp.int32)
    per_step = min(item_count, max(1, 512 // sub_length))
    step_count = item_count // per_step
    key_len = list_len * BLOCK

    def group_step(grad_acc, group_data):
        query_group, grad_group, fetch_group, canon_group, mask_group = group_data
        fetch_table = (fetch_group.reshape(-1)[:, None] == unit_iota[None, :]).astype(jnp.bfloat16)
        gathered = (
            jnp.dot(fetch_table, keys_units, preferred_element_type=jnp.float32)
            .astype(jnp.bfloat16)
            .reshape(per_step, key_len, 2 * HEAD_SIZE)
        )
        key_group = gathered[:, :, :HEAD_SIZE]
        value_group = gathered[:, :, HEAD_SIZE:]
        scores = (
            jnp.einsum("nqd,nkd->nqk", query_group, key_group, preferred_element_type=jnp.float32)
            * score_scale
        )
        masked = jnp.where(mask_group, scores, -1e30)
        row_max = jnp.max(masked, axis=2, keepdims=True)
        row_sum = jnp.sum(
            jnp.where(mask_group, jnp.exp(masked - row_max), 0.0), axis=2, keepdims=True
        )
        log_sum = row_max + jnp.log(row_sum)
        weights = jnp.where(mask_group, jnp.exp(masked - log_sum), 0.0)
        weights_low = weights.astype(jnp.bfloat16)
        out_group = jnp.einsum(
            "nqk,nkd->nqd", weights_low, value_group, preferred_element_type=jnp.float32
        ).astype(jnp.bfloat16)
        row_dot = jnp.sum(
            grad_group.astype(jnp.float32) * out_group.astype(jnp.float32), axis=2, keepdims=True
        )
        grad_weights = jnp.einsum(
            "nqd,nkd->nqk", grad_group, value_group, preferred_element_type=jnp.float32
        )
        score_grad = (weights * (grad_weights - row_dot) * score_scale).astype(jnp.bfloat16)
        query_group_grad = jnp.einsum(
            "nqk,nkd->nqd", score_grad, key_group, preferred_element_type=jnp.float32
        ).astype(jnp.bfloat16)
        key_portion = jnp.einsum(
            "nqk,nqd->nkd", score_grad, query_group, preferred_element_type=jnp.float32
        )
        value_portion = jnp.einsum(
            "nqk,nqd->nkd", weights_low, grad_group, preferred_element_type=jnp.float32
        )
        both_parts = jnp.concatenate([key_portion, value_portion], axis=2).reshape(
            per_step * unit_count, unit_len * 2 * HEAD_SIZE
        )
        place_table = (canon_group.reshape(-1)[:, None] == unit_iota[None, :]).astype(jnp.float32)
        grad_acc = grad_acc + jnp.dot(
            place_table.T,
            both_parts,
            preferred_element_type=jnp.float32,
            precision=lax.Precision.HIGHEST,
        )
        return (grad_acc, (out_group, query_group_grad))

    empty_grad = jnp.zeros((units_total, unit_len * 2 * HEAD_SIZE), jnp.float32)
    scan_inputs = (
        query_items.reshape(step_count, per_step, sub_length, HEAD_SIZE),
        grad_items.reshape(step_count, per_step, sub_length, HEAD_SIZE),
        canon_units.reshape(step_count, per_step, unit_count),
        canon_units.reshape(step_count, per_step, unit_count),
        allowed.reshape(step_count, per_step, sub_length, key_len),
    )
    unit_grads, item_outputs = lax.scan(group_step, empty_grad, scan_inputs)
    kv_grad_all = unit_grads.reshape(total_tokens, 2 * HEAD_SIZE)
    out_items = (
        item_outputs[0]
        .reshape(heads_dev, ulysses_width, sub_count, sub_length, HEAD_SIZE)
        .transpose(1, 2, 3, 0, 4)
        .reshape(ulysses_width * segment_length, 1, head_width)
    )
    qgrad_items = (
        item_outputs[1]
        .reshape(heads_dev, ulysses_width, sub_count, sub_length, HEAD_SIZE)
        .transpose(1, 2, 3, 0, 4)
        .reshape(ulysses_width * segment_length, 1, head_width)
    )
    attended_back, qgrad_back = (
        lax.all_to_all(out_items, "uly", split_axis=0, concat_axis=1, tiled=True),
        lax.all_to_all(qgrad_items, "uly", split_axis=0, concat_axis=1, tiled=True),
    )
    attended = attended_back.reshape(segment_length, ulysses_width * head_width)
    query_grad = qgrad_back.reshape(segment_length, ulysses_width * head_width)
    owned = lax.psum_scatter(kv_grad_all, "blk", scatter_dimension=0, tiled=True)
    result_tuple = lax.all_to_all(
        owned.reshape(ulysses_width * segment_length, 1, 2 * HEAD_SIZE),
        "uly",
        split_axis=0,
        concat_axis=1,
        tiled=True,
    )
    summed_total = result_tuple.reshape(
        segment_length, KEY_VALUE_HEADS, copy_count, 2 * HEAD_SIZE
    ).sum(axis=2)
    gradient_keys = (
        summed_total[:, :, :HEAD_SIZE]
        .reshape(segment_length, KEY_VALUE_HEADS * HEAD_SIZE)
        .astype(jnp.bfloat16)
    )
    gradient_values = (
        summed_total[:, :, HEAD_SIZE:]
        .reshape(segment_length, KEY_VALUE_HEADS * HEAD_SIZE)
        .astype(jnp.bfloat16)
    )
    return (attended, query_grad, gradient_keys, gradient_values)


def solution(mesh):
    in_specs = (
        P(("uly", "blk"), None),
        P(("uly", "blk"), None),
        P(("uly", "blk"), None),
        P(("uly", "blk"), None),
        P("uly", None, None),
    )
    out_specs = (
        P(("uly", "blk"), None),
        P(("uly", "blk"), None),
        P(("uly", "blk"), None),
        P(("uly", "blk"), None),
    )
    return jax.shard_map(body, mesh=mesh, in_specs=in_specs, out_specs=out_specs, check_vma=False)
```

profile of v0, /device:TPU:0, one launch (start us, length us, event | category | flops | bytes accessed | tf_op | source)
XLA Modules:
  0.0 419.6 jit_solution(4855047830497179188)
XLA Ops:
  7.2 0.8 reshape.298
  8.0 0.8 reshape.299
  8.9 13.9 %all_to_all.90 = bf16[64,8,256]{2,0,1:T(8,128)(2,1)} all-to-all(bf16[64,8,256]{2,0,1:T(8,128)(2,1)S(1)} %bitcast.151), channel_id=1, replica_groups=mesh['uly'=8,'blk'=32] {'uly'}, dimensions={1} | all-to-all | bytes 524288 | tf_op jit(solution)/shard_map/all_to_all | solution.py:41
  22.8 1.7 copy.123
  24.4 3.4 all-to-all-start
  27.9 0.8 copy.88
  28.8 0.6 gather_fusion
  29.8 0.1 fusion.46
  30.4 1.7 copy.122
  32.1 4.5 %all-to-all-done = bf16[64,8,256]{2,0,1:T(8,128)(2,1)S(1)} async-done(((bf16[64,8,256]{2,0,1:T(8,128)(2,1)}), bf16[64,8,256]{2,0,1:T(8,128)(2,1)S(1)}, u32[]{:S(2)}, u32[]{:S(2)}) %all-to-all-start) | async-done | bytes 262176 | tf_op jit(solution)/shard_map/all_to_all | solution.py:40
  36.5 3.4 all-to-all-start.2
  40.0 1.0 compare_and_fusion
  41.1 9.5 %all-to-all-done.2 = bf16[64,8,256]{2,0,1:T(8,128)(2,1)S(1)} async-done(((bf16[64,8,256]{2,0,1:T(8,128)(2,1)}), bf16[64,8,256]{2,0,1:T(8,128)(2,1)S(1)}, u32[]{:S(2)}, u32[]{:S(2)}) %all-to-all-start.2) | async-done | bytes 262176 | tf_op jit(solution)/shard_map/all_to_all | solution.py:42
  50.7 42.7 %all-gather.2.cloned.1.call-done = bf16[16384,256]{1,0:T(8,128)(2,1)} async-done(((bf16[512,256]{1,0:T(8,128)(2,1)}), bf16[16384,256]{1,0:T(8,128)(2,1)}) %all-gather.2.cloned.1.call-update) | async-done | bytes 8388624 | tf_op jit(solution)/shard_map/all_gather | solution.py:44
  93.3 13.5 %reshape.301 = bf16[256,16384]{1,0:T(8,128)(2,1)} reshape(bf16[16384,256]{1,0:T(8,128)(2,1)} %all-gather.2.cloned.1.call-done) | data formatting | bytes 16777216 | tf_op jit(solution)/shard_map/reshape | solution.py:82
  106.8 124.2 %while.16 = (s32[]{:T(128)}, f32[256,16384]{1,0:T(8,128)}, bf16[2,8,64,128]{3,2,1,0:T(8,128)(2,1)S(1)}, bf16[2,8,64,128]{3,2,1,0:T(8,128)(2,1)S(1)}, s32[2,8,16]...) while((s32[]{:T(128)}, f32[256,16384]{1,0:T(8,128)}, ...), condition=%wide.region_5.6_spmd.clone, body=%wide.region_1.5_spmd.clone.sunk | while | flops 8343976960 | bytes 164273328 | solution.py:149
  106.9 6.7 %convolution_convert_fusion.2 = bf16[128,16384]{1,0:T(8,128)(2,1)} fusion(bf16[256,16384]{1,0:T(8,128)(2,1)} %get-tuple-element.291, s32[128]{0:T(128)S(1)} %eq.82), kind=kOutput, calls=%fused_computation.3.clone.1 | convolution fusion | flops 1075871744 | bytes 12583424 | tf_op jit(solution)/shard_map/while/body/eval_jaxpr/dot_general | solution.py:92
  113.5 7.4 %reshape.329 = bf16[8,1024,256]{2,1,0:T(8,128)(2,1)} reshape(bf16[128,16384]{1,0:T(8,128)(2,1)} %convolution_convert_fusion.2) | data formatting | bytes 8388608 | tf_op jit(solution)/shard_map/while/body/eval_jaxpr/reshape | solution.py:94
  120.9 2.7 fusion.88
  123.6 0.6 select_reduce_fusion.2
  124.3 0.7 multiply_reduce_fusion.2
  125.0 1.0 multiply_convert_fusion.2
  126.0 0.5 fusion.91
  126.5 0.8 fusion.89
  127.4 0.8 fusion.90
  128.1 4.1 pad_maximum_fusion.3
  132.2 9.1 %copy.125 = f32[8,1024,256]{2,1,0:T(8,128)} copy(f32[8,1024,256]{1,2,0:T(8,128)} %pad_maximum_fusion.3) | data formatting | bytes 16777216 | tf_op jit(solution)/shard_map/while/body/eval_jaxpr/concatenate | solution.py:129
  141.3 9.4 %reshape.330 = f32[128,16384]{1,0:T(8,128)} reshape(f32[8,1024,256]{2,1,0:T(8,128)} %copy.125) | data formatting | bytes 16777216 | tf_op jit(solution)/shard_map/while/body/eval_jaxpr/reshape | solution.py:129
  150.7 17.0 %convolution_add_fusion.2 = f32[256,16384]{1,0:T(8,128)} fusion(f32[128,16384]{1,0:T(8,128)} %reshape.330, f32[256,16384]{1,0:T(8,128)} %get-tuple-element.274, pred[]{:T(512)S(6)} %compare.31, s32[128]{0:T(128)S(1)} %eq.82), kind=kOutput, calls=%fused_computation.2.clone.1 | convolution fusion | flops 6450872320 | bytes 41943552 | tf_op jit(solution)/shard_map/while/body/eval_jaxpr/dot_general | solution.py:133
  167.8 6.7 %convolution_convert_fusion.2 = bf16[128,16384]{1,0:T(8,128)(2,1)} fusion(bf16[256,16384]{1,0:T(8,128)(2,1)} %get-tuple-element.291, s32[128]{0:T(128)S(1)} %eq.82), kind=kOutput, calls=%fused_computation.3.clone.1 | convolution fusion | flops 1075871744 | bytes 12583424 | tf_op jit(solution)/shard_map/while/body/eval_jaxpr/dot_general | solution.py:92
  174.4 7.4 %reshape.329 = bf16[8,1024,256]{2,1,0:T(8,128)(2,1)} reshape(bf16[128,16384]{1,0:T(8,128)(2,1)} %convolution_convert_fusion.2) | data formatting | bytes 8388608 | tf_op jit(solution)/shard_map/while/body/eval_jaxpr/reshape | solution.py:94
  181.8 2.7 fusion.88
  184.5 0.6 select_reduce_fusion.2
  185.1 0.7 multiply_reduce_fusion.2
  185.9 1.0 multiply_convert_fusion.2
  186.9 0.5 fusion.91
  187.4 0.8 fusion.89
  188.3 0.8 fusion.90
  189.0 4.1 pad_maximum_fusion.3
  193.1 9.1 %copy.125 = f32[8,1024,256]{2,1,0:T(8,128)} copy(f32[8,1024,256]{1,2,0:T(8,128)} %pad_maximum_fusion.3) | data formatting | bytes 16777216 | tf_op jit(solution)/shard_map/while/body/eval_jaxpr/concatenate | solution.py:129
  202.2 9.4 %reshape.330 = f32[128,16384]{1,0:T(8,128)} reshape(f32[8,1024,256]{2,1,0:T(8,128)} %copy.125) | data formatting | bytes 16777216 | tf_op jit(solution)/shard_map/while/body/eval_jaxpr/reshape | solution.py:129
  211.6 19.4 %convolution_add_fusion.2 = f32[256,16384]{1,0:T(8,128)} fusion(f32[128,16384]{1,0:T(8,128)} %reshape.330, f32[256,16384]{1,0:T(8,128)} %get-tuple-element.274, pred[]{:T(512)S(6)} %compare.31, s32[128]{0:T(128)S(1)} %eq.82), kind=kOutput, calls=%fused_computation.2.clone.1 | convolution fusion | flops 6450872320 | bytes 41943552 | tf_op jit(solution)/shard_map/while/body/eval_jaxpr/dot_general | solution.py:133
  231.0 18.0 %reshape.310 = f32[16384,256]{1,0:T(8,128)} reshape(f32[256,16384]{1,0:T(8,128)} %get-tuple-element.86) | data formatting | bytes 33554432 | tf_op jit(solution)/shard_map/reshape | solution.py:150
  249.0 0.3 copy.102
  249.3 0.1 reshape.322
  249.4 0.5 broadcast.438
  249.9 2.2 reduce.1
  252.2 0.8 reshape.325
  252.9 6.9 %all-to-all-start.4 = ((bf16[8,2,8192]{2,1,0:T(2,128)(2,1)}), bf16[8,2,8192]{2,1,0:T(2,128)(2,1)S(1)}, u32[]{:S(2)}, u32[]{:S(2)}) async-start(bf16[8,2,8192]{2,1,0:T(2,128)(2,1)} %reshape.325), calls=%async_computation.4 | async-start | bytes 524288 | tf_op jit(solution)/shard_map/all_to_all | solution.py:165
  259.8 0.3 copy.99
  260.1 0.1 reshape.321
  260.2 2.2 reduce
  262.4 0.8 reshape.323
  263.2 11.2 %all-to-all-done.4 = bf16[8,2,8192]{2,1,0:T(2,128)(2,1)S(1)} async-done(((bf16[8,2,8192]{2,1,0:T(2,128)(2,1)}), bf16[8,2,8192]{2,1,0:T(2,128)(2,1)S(1)}, u32[]{:S(2)}, u32[]{:S(2)}) %all-to-all-start.4) | async-done | bytes 262176 | tf_op jit(solution)/shard_map/all_to_all | solution.py:165
  274.4 3.4 all-to-all-start.3
  277.8 115.9 %reduce-scatter.2.cloned.1.call-done = f32[512,256]{1,0:T(8,128)} async-done(((f32[16384,256]{1,0:T(8,128)}), f32[512,256]{1,0:T(8,128)}) %reduce-scatter.2.cloned.1.call-update) | async-done | bytes 524304 | tf_op jit(solution)/shard_map/reduce_scatter | solution.py:169
  393.7 2.2 reshape.311
  396.0 6.3 %all-to-all-start.5 = ((f32[512,1,256]{2,1,0:T(1,128)}), f32[512,1,256]{2,1,0:T(1,128)S(1)}, u32[]{:S(2)}, u32[]{:S(2)}) async-start(f32[512,1,256]{2,1,0:T(1,128)} %reshape.311), calls=%async_computation.6 | async-start | bytes 1048576 | tf_op jit(solution)/shard_map/all_to_all | solution.py:170
  402.2 0.3 reshape.326
  402.5 0.7 copy.115
  403.3 0.3 reshape.324
  403.6 0.7 copy.114
  404.3 7.7 %all-to-all-done.5 = f32[512,1,256]{2,1,0:T(1,128)S(1)} async-done(((f32[512,1,256]{2,1,0:T(1,128)}), f32[512,1,256]{2,1,0:T(1,128)S(1)}, u32[]{:S(2)}, u32[]{:S(2)}) %all-to-all-start.5) | async-done | bytes 524320 | tf_op jit(solution)/shard_map/all_to_all | solution.py:170
  412.1 0.6 copy_bitcast_fusion.2
  (53 shorter events, 1.7 us)
Async XLA Ops:
  7.2 86.2 %all-gather.2.cloned.1.call-start = ((), (), s32[]{:S(2)}) async-start(), calls=%async_computation.7 | async-start | bytes 8650752 | tf_op jit(solution)/shard_map/all_gather | solution.py:44
  24.4 12.1 %all-to-all-start = ((bf16[64,8,256]{2,0,1:T(8,128)(2,1)}), bf16[64,8,256]{2,0,1:T(8,128)(2,1)S(1)}, u32[]{:S(2)}, u32[]{:S(2)}) async-start(bf16[64,8,256]{2,0,1:T(8,128)(2,1)} %bitcast.115), calls=%async_computation | async-start | bytes 524288 | tf_op jit(solution)/shard_map/all_to_all | solution.py:40
  36.5 14.0 %all-to-all-start.2 = ((bf16[64,8,256]{2,0,1:T(8,128)(2,1)}), bf16[64,8,256]{2,0,1:T(8,128)(2,1)S(1)}, u32[]{:S(2)}, u32[]{:S(2)}) async-start(bf16[64,8,256]{2,0,1:T(8,128)(2,1)} %bitcast.114), calls=%async_computation.2 | async-start | bytes 524288 | tf_op jit(solution)/shard_map/all_to_all | solution.py:42
  39.9 353.8 %reduce-scatter.2.cloned.1.call-start = ((), (), s32[]{:S(2)}) async-start(), calls=%async_computation.8 | async-start | bytes 17301504 | tf_op jit(solution)/shard_map/reduce_scatter | solution.py:169
  120.9 3.3 copy-start
  181.8 3.3 copy-start
  252.9 21.5 %all-to-all-start.4 = ((bf16[8,2,8192]{2,1,0:T(2,128)(2,1)}), bf16[8,2,8192]{2,1,0:T(2,128)(2,1)S(1)}, u32[]{:S(2)}, u32[]{:S(2)}) async-start(bf16[8,2,8192]{2,1,0:T(2,128)(2,1)} %reshape.325), calls=%async_computation.4 | async-start | bytes 524288 | tf_op jit(solution)/shard_map/all_to_all | solution.py:165
  274.4 121.5 %all-to-all-start.3 = ((bf16[8,2,8192]{2,1,0:T(2,128)(2,1)}), bf16[8,2,8192]{2,1,0:T(2,128)(2,1)S(1)}, u32[]{:S(2)}, u32[]{:S(2)}) async-start(bf16[8,2,8192]{2,1,0:T(2,128)(2,1)} %reshape.323), calls=%async_computation.3 | async-start | bytes 524288 | tf_op jit(solution)/shard_map/all_to_all | solution.py:164
  396.0 16.0 %all-to-all-start.5 = ((f32[512,1,256]{2,1,0:T(1,128)}), f32[512,1,256]{2,1,0:T(1,128)S(1)}, u32[]{:S(2)}, u32[]{:S(2)}) async-start(f32[512,1,256]{2,1,0:T(1,128)} %reshape.311), calls=%async_computation.6 | async-start | bytes 1048576 | tf_op jit(solution)/shard_map/all_to_all | solution.py:170
Sparse Core Ops, SparseCore 0:
  22.9 70.4 all-gather.1
  249.1 144.5 reduce-scatter.1
where the time goes:
time: 422 us; the launch traced here: 420 us
  waiting for transfers between devices  191 us (45%)
  local copies, waits for them, and re-layouts  98.5 us (23%)
  matrix products  62.6 us (15%)
  starting transfers between devices  23.5 us (6%)
  other arithmetic  15.2 us (4%)
  between operations  14.3 us (3%)
  blocking collectives  13.9 us (3%)
    reduce_scatter x1, waiting for transfers between devices, body(): lax.psum_scatter(kv_grad_all, 'blk', scatter_dimension=0, tiled=True)  116 us
    all_gather x1, waiting for transfers between devices, body(): keys_all = lax.all_gather(kv_mine[:, 0, :], 'blk', axis=0, tiled=True)  42.7 us
    dot_general x2, matrix products, group_step(): jnp.dot(place_table.T, both_parts, preferred_element_type=jnp.float32, pr...  36.4 us
    reshape x2, local copies, waits for them, and re-layouts, group_step(): jnp.concatenate([key_portion, value_portion], axis=2)  18.8 us
    concatenate x2, local copies, waits for them, and re-layouts, group_step(): jnp.concatenate([key_portion, value_portion], axis=2)  18.2 us
    reshape x1, local copies, waits for them, and re-layouts, body(): kv_grad_all = unit_grads.reshape(total_tokens, 2 * HEAD_SIZE)  18 us
    reshape x2, local copies, waits for them, and re-layouts, group_step(): gathered = jnp.dot(fetch_table, keys_units, preferred_element_type=jnp.fl...  14.8 us
    all_to_all x1, blocking collectives, body(): lax.all_to_all(kv_slots, 'uly', split_axis=1, concat_axis=0, tiled=True)  13.9 us
  transfers between devices with their start and end apart: 7, of which 6 were waited for; matrix products, arithmetic and copies ran while one was open for 4% of the time, Pallas kernels for 0%

commit v1 on v0

--- a/solution.py
+++ b/solution.py
@@ -41,7 +41,9 @@
         lax.all_to_all(kv_slots, "uly", split_axis=1, concat_axis=0, tiled=True),
         lax.all_to_all(grad_slots, "uly", split_axis=1, concat_axis=0, tiled=True),
     )
-    keys_all = lax.all_gather(kv_mine[:, 0, :], "blk", axis=0, tiled=True)
+    keys_all = jnp.concatenate(
+        lax.all_to_all(jnp.stack([kv_mine[:, 0, :]] * lax.axis_size("blk")), "blk", 0, 0), axis=0
+    )
     item_count = heads_dev * ulysses_width * sub_count
     query_items = (
         query_all.reshape(ulysses_width, sub_count, sub_length, heads_dev, HEAD_SIZE)

time: 422 us -> 574 us (1.36)
  waiting for transfers between devices: 191 us -> 334 us
  starting transfers between devices: 23.5 us -> 30.6 us
    all_to_all x1 -> x2, waiting for transfers between devices: 9.48 us -> 190 us  [the longest x1 183 us: body(): lax.all_to_all(jnp.stack([kv_mine[:, 0, :]] * lax.axis_size('blk')), 'blk...]
    all_gather x1 -> x0, waiting for transfers between devices: 42.7 us -> none  [body(): keys_all = lax.all_gather(kv_mine[:, 0, :], 'blk', axis=0, tiled=True)]
    another operation x0 -> x2, local copies, waits for them, and re-layouts: none -> 17.6 us  [the longest x1 13.5 us: body(): keys_units = keys_all.reshape(units_total, unit_len * 2 * HEAD_SIZE)]
    reshape x1 -> x0, local copies, waits for them, and re-layouts: 13.5 us -> none  [body(): keys_units = keys_all.reshape(units_total, unit_len * 2 * HEAD_SIZE)]
    all_to_all x1 -> x2, starting transfers between devices: 3.41 us -> 14.4 us  [the longest x1 9.15 us: body(): lax.all_to_all(jnp.stack([kv_mine[:, 0, :]] * lax.axis_size('blk')), 'blk...]
    reduce_scatter x1, waiting for transfers between devices: 116 us -> 124 us  [body(): lax.psum_scatter(kv_grad_all, 'blk', scatter_dimension=0, tiled=True)]
    all_to_all x1, waiting for transfers between devices: 11.2 us -> 5.29 us  [body(): lax.all_to_all(qgrad_items, 'uly', split_axis=0, concat_axis=1, tiled=True)]
  transfers between devices with their start and end apart: 7 -> 7, of which waited for: 6 -> 6; matrix products, arithmetic and copies ran while one was open for 4% -> 3% of each run, Pallas kernels for 0% -> 0%
where the time goes in v1:
time: 574 us; the launch traced here: 570 us
  waiting for transfers between devices  334 us (58%)
  local copies, waits for them, and re-layouts  102 us (18%)
  matrix products  62.6 us (11%)
  starting transfers between devices  30.6 us (5%)
  other arithmetic  15.3 us (3%)
  between operations  14.3 us (2%)
  blocking collectives  11.3 us (2%)
    all_to_all x1, waiting for transfers between devices, body(): lax.all_to_all(jnp.stack([kv_mine[:, 0, :]] * lax.axis_size('blk')), 'blk...  183 us
    reduce_scatter x1, waiting for transfers between devices, body(): lax.psum_scatter(kv_grad_all, 'blk', scatter_dimension=0, tiled=True)  124 us
    dot_general x2, matrix products, group_step(): jnp.dot(place_table.T, both_parts, preferred_element_type=jnp.float32, pr...  36.4 us
    reshape x2, local copies, waits for them, and re-layouts, group_step(): jnp.concatenate([key_portion, value_portion], axis=2)  18.8 us
    concatenate x2, local copies, waits for them, and re-layouts, group_step(): jnp.concatenate([key_portion, value_portion], axis=2)  18.2 us
    reshape x1, local copies, waits for them, and re-layouts, body(): kv_grad_all = unit_grads.reshape(total_tokens, 2 * HEAD_SIZE)  18 us
    reshape x2, local copies, waits for them, and re-layouts, group_step(): gathered = jnp.dot(fetch_table, keys_units, preferred_element_type=jnp.fl...  14.8 us
    another operation x1, local copies, waits for them, and re-layouts, body(): keys_units = keys_all.reshape(units_total, unit_len * 2 * HEAD_SIZE)  13.5 us
  transfers between devices with their start and end apart: 7, of which 6 were waited for; matrix products, arithmetic and copies ran while one was open for 3% of the time, Pallas kernels for 0%

profile of v1, /device:TPU:0, one launch (start us, length us, event | category | flops | bytes accessed | tf_op | source)
XLA Modules:
  0.0 570.4 jit_solution(607451402119821147)
XLA Ops:
  7.2 0.8 reshape.297
  7.9 0.8 reshape.298
  8.8 0.7 broadcast_in_dim.53
  9.5 5.2 all-to-all-start.1
  14.7 1.7 copy.123
  16.4 7.1 %all-to-all-done.1 = bf16[64,8,256]{2,0,1:T(8,128)(2,1)S(1)} async-done(((bf16[64,8,256]{2,0,1:T(8,128)(2,1)}), bf16[64,8,256]{2,0,1:T(8,128)(2,1)S(1)}, u32[]{:S(2)}, u32[]{:S(2)}) %all-to-all-start.1) | async-done | bytes 262176 | tf_op jit(solution)/shard_map/all_to_all | solution.py:41
  23.5 3.4 all-to-all-start
  26.9 1.0 copy.122
  27.9 7.7 %all-to-all-done = bf16[64,8,256]{2,0,1:T(8,128)(2,1)S(1)} async-done(((bf16[64,8,256]{2,0,1:T(8,128)(2,1)}), bf16[64,8,256]{2,0,1:T(8,128)(2,1)S(1)}, u32[]{:S(2)}, u32[]{:S(2)}) %all-to-all-start) | async-done | bytes 262176 | tf_op jit(solution)/shard_map/all_to_all | solution.py:40
  35.6 11.3 %all_to_all.95 = bf16[64,8,256]{2,0,1:T(8,128)(2,1)S(1)} all-to-all(bf16[64,8,256]{2,0,1:T(8,128)(2,1)S(1)} %bitcast.154), channel_id=1, replica_groups=mesh['uly'=8,'blk'=32] {'uly'}, dimensions={1} | all-to-all | bytes 524288 | tf_op jit(solution)/shard_map/all_to_all | solution.py:42
  46.8 4.2 stack.3
  51.0 9.1 %all-to-all-start.2 = ((bf16[32,512,256]{2,1,0:T(8,128)(2,1)}), bf16[32,512,256]{2,1,0:T(8,128)(2,1)}, u32[]{:S(2)}, u32[]{:S(2)}) async-start(bf16[32,512,256]{2,1,0:T(8,128)(2,1)} %stack.3), calls=%async_computation.2 | async-start | bytes 16777216 | tf_op jit(solution)/shard_map/all_to_all | solution.py:45
  60.5 0.6 gather_fusion
  62.1 1.0 compare_and_fusion
  63.3 183.0 %all-to-all-done.2 = bf16[32,512,256]{2,1,0:T(8,128)(2,1)} async-done(((bf16[32,512,256]{2,1,0:T(8,128)(2,1)}), bf16[32,512,256]{2,1,0:T(8,128)(2,1)}, u32[]{:S(2)}, u32[]{:S(2)}) %all-to-all-start.2) | async-done | bytes 8388640 | tf_op jit(solution)/shard_map/all_to_all | solution.py:45
  246.3 13.5 %reshape_reshape.10 = bf16[256,16384]{1,0:T(8,128)(2,1)} reshape(bf16[32,512,256]{2,1,0:T(8,128)(2,1)} %all-to-all-done.2) | data formatting | bytes 16777216 | tf_op jit(solution)/shard_map/reshape;reshape | solution.py:84
  259.8 124.2 %while.16 = (s32[]{:T(128)}, f32[256,16384]{1,0:T(8,128)}, bf16[2,8,64,128]{3,2,1,0:T(8,128)(2,1)S(1)}, bf16[2,8,64,128]{3,2,1,0:T(8,128)(2,1)S(1)}, s32[2,8,16]...) while((s32[]{:T(128)}, f32[256,16384]{1,0:T(8,128)}, ...), condition=%wide.region_5.6_spmd.clone, body=%wide.region_1.5_spmd.clone.sunk | while | flops 8343976960 | bytes 164273328 | solution.py:151
  259.8 6.7 %convolution_convert_fusion.2 = bf16[128,16384]{1,0:T(8,128)(2,1)} fusion(bf16[256,16384]{1,0:T(8,128)(2,1)} %get-tuple-element.291, s32[128]{0:T(128)S(1)} %eq.82), kind=kOutput, calls=%fused_computation.3.clone.1 | convolution fusion | flops 1075871744 | bytes 12583424 | tf_op jit(solution)/shard_map/while/body/eval_jaxpr/dot_general | solution.py:94
  266.5 7.4 %reshape.327 = bf16[8,1024,256]{2,1,0:T(8,128)(2,1)} reshape(bf16[128,16384]{1,0:T(8,128)(2,1)} %convolution_convert_fusion.2) | data formatting | bytes 8388608 | tf_op jit(solution)/shard_map/while/body/eval_jaxpr/reshape | solution.py:96
  273.9 2.7 fusion.88
  276.6 0.6 select_reduce_fusion.2
  277.2 0.7 multiply_reduce_fusion.2
  278.0 1.0 multiply_convert_fusion.2
  279.0 0.5 fusion.91
  279.5 0.8 fusion.89
  280.3 0.8 fusion.90
  281.1 4.1 pad_maximum_fusion.3
  285.1 9.1 %copy.125 = f32[8,1024,256]{2,1,0:T(8,128)} copy(f32[8,1024,256]{1,2,0:T(8,128)} %pad_maximum_fusion.3) | data formatting | bytes 16777216 | tf_op jit(solution)/shard_map/while/body/eval_jaxpr/concatenate | solution.py:131
  294.3 9.4 %reshape.328 = f32[128,16384]{1,0:T(8,128)} reshape(f32[8,1024,256]{2,1,0:T(8,128)} %copy.125) | data formatting | bytes 16777216 | tf_op jit(solution)/shard_map/while/body/eval_jaxpr/reshape | solution.py:131
  303.6 17.0 %convolution_add_fusion.2 = f32[256,16384]{1,0:T(8,128)} fusion(f32[128,16384]{1,0:T(8,128)} %reshape.328, f32[256,16384]{1,0:T(8,128)} %get-tuple-element.274, pred[]{:T(512)S(6)} %compare.31, s32[128]{0:T(128)S(1)} %eq.82), kind=kOutput, calls=%fused_computation.2.clone.1 | convolution fusion | flops 6450872320 | bytes 41943552 | tf_op jit(solution)/shard_map/while/body/eval_jaxpr/dot_general | solution.py:135
  320.7 6.7 %convolution_convert_fusion.2 = bf16[128,16384]{1,0:T(8,128)(2,1)} fusion(bf16[256,16384]{1,0:T(8,128)(2,1)} %get-tuple-element.291, s32[128]{0:T(128)S(1)} %eq.82), kind=kOutput, calls=%fused_computation.3.clone.1 | convolution fusion | flops 1075871744 | bytes 12583424 | tf_op jit(solution)/shard_map/while/body/eval_jaxpr/dot_general | solution.py:94
  327.4 7.4 %reshape.327 = bf16[8,1024,256]{2,1,0:T(8,128)(2,1)} reshape(bf16[128,16384]{1,0:T(8,128)(2,1)} %convolution_convert_fusion.2) | data formatting | bytes 8388608 | tf_op jit(solution)/shard_map/while/body/eval_jaxpr/reshape | solution.py:96
  334.8 2.7 fusion.88
  337.4 0.6 select_reduce_fusion.2
  338.1 0.7 multiply_reduce_fusion.2
  338.9 1.0 multiply_convert_fusion.2
  339.9 0.5 fusion.91
  340.4 0.8 fusion.89
  341.2 0.8 fusion.90
  342.0 4.1 pad_maximum_fusion.3
  346.0 9.1 %copy.125 = f32[8,1024,256]{2,1,0:T(8,128)} copy(f32[8,1024,256]{1,2,0:T(8,128)} %pad_maximum_fusion.3) | data formatting | bytes 16777216 | tf_op jit(solution)/shard_map/while/body/eval_jaxpr/concatenate | solution.py:131
  355.1 9.4 %reshape.328 = f32[128,16384]{1,0:T(8,128)} reshape(f32[8,1024,256]{2,1,0:T(8,128)} %copy.125) | data formatting | bytes 16777216 | tf_op jit(solution)/shard_map/while/body/eval_jaxpr/reshape | solution.py:131
  364.5 19.4 %convolution_add_fusion.2 = f32[256,16384]{1,0:T(8,128)} fusion(f32[128,16384]{1,0:T(8,128)} %reshape.328, f32[256,16384]{1,0:T(8,128)} %get-tuple-element.274, pred[]{:T(512)S(6)} %compare.31, s32[128]{0:T(128)S(1)} %eq.82), kind=kOutput, calls=%fused_computation.2.clone.1 | convolution fusion | flops 6450872320 | bytes 41943552 | tf_op jit(solution)/shard_map/while/body/eval_jaxpr/dot_general | solution.py:135
  383.9 18.0 %reshape.308 = f32[16384,256]{1,0:T(8,128)} reshape(f32[256,16384]{1,0:T(8,128)} %get-tuple-element.86) | data formatting | bytes 33554432 | tf_op jit(solution)/shard_map/reshape | solution.py:152
  401.9 0.3 copy.102
  402.2 0.1 reshape.320
  402.4 0.5 broadcast.439
  402.9 2.2 reduce.1
  405.1 0.8 reshape.323
  405.9 3.4 all-to-all-start.5
  409.3 0.3 copy.99
  409.7 2.2 reduce
  411.9 0.8 reshape.321
  412.7 5.3 all-to-all-done.5
  418.0 3.4 all-to-all-start.4
  421.4 123.5 %reduce-scatter.2.cloned.1.call-done = f32[512,256]{1,0:T(8,128)} async-done(((f32[16384,256]{1,0:T(8,128)}), f32[512,256]{1,0:T(8,128)}) %reduce-scatter.2.cloned.1.call-update) | async-done | bytes 524304 | tf_op jit(solution)/shard_map/reduce_scatter | solution.py:171
  544.9 2.2 reshape.309
  547.1 5.9 %all-to-all-start.6 = ((f32[512,1,256]{2,1,0:T(1,128)}), f32[512,1,256]{2,1,0:T(1,128)S(1)}, u32[]{:S(2)}, u32[]{:S(2)}) async-start(f32[512,1,256]{2,1,0:T(1,128)} %reshape.309), calls=%async_computation.7 | async-start | bytes 1048576 | tf_op jit(solution)/shard_map/all_to_all | solution.py:172
  553.1 0.3 reshape.324
  553.4 0.7 copy.115
  554.1 0.3 reshape.322
  554.4 0.7 copy.114
  555.2 7.7 %all-to-all-done.6 = f32[512,1,256]{2,1,0:T(1,128)S(1)} async-done(((f32[512,1,256]{2,1,0:T(1,128)}), f32[512,1,256]{2,1,0:T(1,128)S(1)}, u32[]{:S(2)}, u32[]{:S(2)}) %all-to-all-start.6) | async-done | bytes 524320 | tf_op jit(solution)/shard_map/all_to_all | solution.py:172
  563.0 0.6 copy_bitcast_fusion.2
  (55 shorter events, 2.0 us)
Async XLA Ops:
  9.5 14.0 %all-to-all-start.1 = ((bf16[64,8,256]{2,0,1:T(8,128)(2,1)}), bf16[64,8,256]{2,0,1:T(8,128)(2,1)S(1)}, u32[]{:S(2)}, u32[]{:S(2)}) async-start(bf16[64,8,256]{2,0,1:T(8,128)(2,1)} %bitcast.6), calls=%async_computation.1 | async-start | bytes 524288 | tf_op jit(solution)/shard_map/all_to_all | solution.py:41
  23.5 12.1 %all-to-all-start = ((bf16[64,8,256]{2,0,1:T(8,128)(2,1)}), bf16[64,8,256]{2,0,1:T(8,128)(2,1)S(1)}, u32[]{:S(2)}, u32[]{:S(2)}) async-start(bf16[64,8,256]{2,0,1:T(8,128)(2,1)} %bitcast.115), calls=%async_computation | async-start | bytes 524288 | tf_op jit(solution)/shard_map/all_to_all | solution.py:40
  51.0 9.3 %copy-start.1 = (s32[2,128,8]{1,2,0:T(8,128)S(1)}, s32[2,128,8]{1,2,0:T(8,128)}, u32[]{:S(2)}) copy-start(s32[2,128,8]{1,2,0:T(8,128)} %param.11) | copy-start | bytes 24580
  51.0 195.3 %all-to-all-start.2 = ((bf16[32,512,256]{2,1,0:T(8,128)(2,1)}), bf16[32,512,256]{2,1,0:T(8,128)(2,1)}, u32[]{:S(2)}, u32[]{:S(2)}) async-start(bf16[32,512,256]{2,1,0:T(8,128)(2,1)} %stack.3), calls=%async_computation.2 | async-start | bytes 16777216 | tf_op jit(solution)/shard_map/all_to_all | solution.py:45
  60.2 484.8 %reduce-scatter.2.cloned.1.call-start = ((), (), s32[]{:S(2)}) async-start(), calls=%async_computation.8 | async-start | bytes 17301504 | tf_op jit(solution)/shard_map/reduce_scatter | solution.py:171
  273.9 3.3 copy-start
  334.8 3.3 copy-start
  405.9 12.1 %all-to-all-start.5 = ((bf16[8,2,8192]{2,1,0:T(2,128)(2,1)}), bf16[8,2,8192]{2,1,0:T(2,128)(2,1)S(1)}, u32[]{:S(2)}, u32[]{:S(2)}) async-start(bf16[8,2,8192]{2,1,0:T(2,128)(2,1)} %reshape.323), calls=%async_computation.5 | async-start | bytes 524288 | tf_op jit(solution)/shard_map/all_to_all | solution.py:167
  418.0 129.1 %all-to-all-start.4 = ((bf16[8,2,8192]{2,1,0:T(2,128)(2,1)}), bf16[8,2,8192]{2,1,0:T(2,128)(2,1)S(1)}, u32[]{:S(2)}, u32[]{:S(2)}) async-start(bf16[8,2,8192]{2,1,0:T(2,128)(2,1)} %reshape.321), calls=%async_computation.4 | async-start | bytes 524288 | tf_op jit(solution)/shard_map/all_to_all | solution.py:166
  547.1 15.7 %all-to-all-start.6 = ((f32[512,1,256]{2,1,0:T(1,128)}), f32[512,1,256]{2,1,0:T(1,128)S(1)}, u32[]{:S(2)}, u32[]{:S(2)}) async-start(f32[512,1,256]{2,1,0:T(1,128)} %reshape.309), calls=%async_computation.7 | async-start | bytes 1048576 | tf_op jit(solution)/shard_map/all_to_all | solution.py:172
Sparse Core Ops, SparseCore 0:
  402.1 142.8 reduce-scatter.1
